TPU v7x, 256 devices: a whole 4x4x8 slice. The times are simulated.
256 devices in a mesh: gx: 8 (over x, core), gy: 32 (over y, z).
Axes of the slice: x: 4, y: 4, z: 8, core: 2. Of those that a mesh axis runs over, the one named last changes fastest.
Arguments:
- cells: bfloat16 [256, 1048576], P(None, ('gx', 'gy')), may hold values from -25 to 25
- send_index: int32 [8192, 2], P(('gx', 'gy')), may hold values from 0 to 31
- send_count: int32 [8192], P(('gx', 'gy')), may hold values from 1 to 2, as said below
- prolong_block: int32 [8192, 4], P(('gx', 'gy')), may hold values from 0 to 63, as said below
- prolong_level: int32 [8192, 4], P(('gx', 'gy')), may hold values from 0 to 3
- prolong_maps: bfloat16 [4, 128, 512], replicated, may hold values from -0.25 to 0.25
Outputs:
- factor: float32 [256, 256], replicated
- modes: float32 [128, 4194304], P(None, ('gx', 'gy'))
Inputs may be any that keep to these rules, and one draw needn't show every extreme that they name: `send_count`: every sender and owner pair uses 1 to 2 slots; some pair uses all 2. `prolong_block`: the first slot feeding each brick is slot 0 of some sender, a multiple of 2.
All inputs are finite; a program needn't handle non-finite values.
Results may differ from a plain program's by a relative error of at most 0.0041.
Values may be sent and summed in bfloat16 or wider, within the bound.
No kernel may reach another device: no remote copies, remote signals or barrier semaphores. Data moves between devices by JAX's collectives and lax.ppermute only.
A program may use at most 128 MiB of HBM per device.

v0:
```python
import jax
import jax.numpy as jnp
from jax import lax
from jax.sharding import PartitionSpec as P

RANK = 128
BLK = 128


def from_partner(value, axis, bit):
    mask = 2**bit
    pairs = [(source, source ^ mask) for source in range(lax.axis_size(axis))]
    return lax.ppermute(value, axis, pairs)


def lift(received, blocks, levels, maps):
    picked = jnp.take(received, blocks, axis=1)
    chosen = jnp.take(maps, levels, axis=0)
    lifted = jnp.einsum("sbnc,bncd->sbd", picked, chosen, preferred_element_type=jnp.float32)
    return lifted.reshape(lifted.shape[0], -1).astype(jnp.bfloat16)


def combined(factor, other):
    mine = jnp.dot(factor, factor.T, precision=lax.Precision.HIGHEST)
    theirs = jnp.dot(other, other.T, precision=lax.Precision.HIGHEST)
    return jnp.linalg.cholesky(mine + theirs)


def body(cells, send_index, send_count, prolong_block, prolong_level, prolong_maps):
    snaps = cells.shape[0]
    local = cells.reshape(snaps, -1, BLK)
    peers, slots = send_index.shape
    outgoing = jnp.take(local, send_index.reshape(-1), axis=1)
    live = (jnp.arange(slots, dtype=jnp.int32)[None, :] < send_count[:, None]).reshape(-1)
    outgoing = outgoing * live[None, :, None].astype(jnp.bfloat16)
    received = lax.all_to_all(outgoing, "gy", split_axis=1, concat_axis=1, tiled=True)
    bricks = lift(received, prolong_block, prolong_level, prolong_maps)
    gram = lax.dot_general(
        bricks, bricks, (((1,), (1,)), ((), ())), preferred_element_type=jnp.float32
    )
    total_cells = lax.axis_size("gx") * lax.axis_size("gy") * bricks.shape[1]
    gram = lax.psum(gram, ("gx", "gy"))
    covariance = gram / total_cells
    factor = jnp.linalg.cholesky(covariance)
    kept = RANK
    modes = lax.linalg.triangular_solve(
        factor[:kept, :kept], bricks[:kept].astype(jnp.float32), left_side=True, lower=True
    )
    return (factor, modes)


def solution(mesh):
    in_specs = (
        P(None, ("gx", "gy")),
        P(("gx", "gy"), None),
        P(("gx", "gy")),
        P(("gx", "gy"), None),
        P(("gx", "gy"), None),
        P(),
    )
    out_specs = (P(), P(None, ("gx", "gy")))
    return jax.shard_map(body, mesh=mesh, in_specs=in_specs, out_specs=out_specs, check_vma=False)
```

profile of v0, /device:TPU:2, one launch (start us, length us, event | category | flops | bytes accessed | tf_op | source)
XLA Modules:
  0.0 478.6 jit_solution(10285981647548982762)
XLA Ops:
  7.2 0.8 copy.35
  8.3 4.1 copy.36
  12.3 3.2 copy.38
  15.8 3.1 gather_fusion.1
  18.9 4.7 multiply_bitcast_fusion
  23.6 11.6 %all-to-all-start = ((bf16[256,64,128]{2,0,1:T(8,128)(2,1)}), bf16[256,64,128]{2,0,1:T(8,128)(2,1)}, u32[]{:S(2)}, u32[]{:S(2)}) async-start(bf16[256,64,128]{2,0,1:T(8,128)(2,1)} %multiply_bitcast_fusion), calls=%async_computation | async-start | bytes 8388608 | tf_op jit(solution)/shard_map/all_to_all | solution.py:36
  35.7 8.1 %gather_fusion = bf16[128,128,512]{2,1,0:T(8,128)(2,1)} fusion(bf16[4,128,512]{2,1,0:T(8,128)(2,1)S(1)} %copy-done, s32[1024]{0:T(1024)S(1)} %pad_clamp_fusion.2), kind=kCustom, calls=%fused_computation | custom fusion | bytes 33554944 | tf_op jit(solution)/shard_map/jit(_take)/gather | solution.py:18
  43.9 22.6 %copy.33 = bf16[32,4,128,512]{2,3,1,0:T(8,128)(2,1)} copy(bf16[32,4,128,512]{3,2,1,0:T(8,128)(2,1)} %bitcast.43) | data formatting | bytes 33554432 | tf_op jit(solution)/shard_map/jit(_take)/gather | solution.py:18
  66.7 65.5 %all-to-all-done = bf16[256,64,128]{2,0,1:T(8,128)(2,1)} async-done(((bf16[256,64,128]{2,0,1:T(8,128)(2,1)}), bf16[256,64,128]{2,0,1:T(8,128)(2,1)}, u32[]{:S(2)}, u32[]{:S(2)}) %all-to-all-start) | async-done | bytes 4194336 | tf_op jit(solution)/shard_map/all_to_all | solution.py:36
  132.2 8.9 %gather_fusion.2 = bf16[128,256,128]{2,1,0:T(8,128)(2,1)} fusion(bf16[256,64,128]{2,0,1:T(8,128)(2,1)} %all-to-all-done, s32[1024]{0:T(1024)S(1)} %pad_clamp_fusion), kind=kCustom, calls=%fused_computation.2 | custom fusion | bytes 16777728 | tf_op jit(solution)/shard_map/jit(_take)/gather | solution.py:17
  141.1 12.8 %fusion.3 = bf16[256,32,512]{0,2,1:T(8,128)(2,1)} fusion(bf16[32,4,256,128]{3,2,1,0:T(8,128)(2,1)} %bitcast.45, pred[32,4]{1,0:T(8,128)(4,1)S(1)} %copy.34, bf16[32,4,128,512]{2,3,1,0:T(8,128)(2,1)} %copy.33, pred[32,4]{1,0:T(8,128)(4,1)S(1)} %copy.31), kind=kOutput, calls=%fused_computation.7 | convolution fusion | flops 4311744512 | bytes 33554688 | tf_op jit(solution)/shard_map/sbnc,bncd->sbd/dot_general | solution.py:19
  154.0 9.8 %convolution_bitcast_fusion = f32[256,256]{0,1:T(8,128)} fusion(bf16[256,32,512]{0,2,1:T(8,128)(2,1)} %fusion.3), kind=kOutput, calls=%fused_computation.14 | convolution fusion | flops 2147483648 | bytes 8650752 | tf_op jit(solution)/shard_map/dot_general | solution.py:38
  163.8 4.6 triangular_solve.20
  168.5 246.3 %all-reduce.3.cloned.1.call-done = f32[256,256]{0,1:T(8,128)} async-done(((f32[256,256]{0,1:T(8,128)}), f32[256,256]{0,1:T(8,128)}) %all-reduce.3.cloned.1.call-update) | async-done | bytes 262160 | tf_op jit(solution)/shard_map/psum | solution.py:42
  414.7 1.0 broadcast_multiply_fusion
  415.8 1.0 fusion.13
  416.9 11.7 %cholesky.53 = f32[128,128]{1,0:T(8,128)S(1)} custom-call(f32[128,128]{1,0:T(8,128)S(1)} %cholesky.124), custom_call_target="Cholesky" | custom-call | tf_op jit(solution)/shard_map/jit(cholesky)/cholesky | solution.py:44
  428.6 9.8 %custom-call.14 = f32[1,128,128]{1,2,0:T(8,128)S(1)} custom-call(f32[1,128,128]{2,1,0:T(8,128)S(1)} %get-tuple-element.5), custom_call_target="InvertDiagBlocksLowerTriangular" | custom-call | tf_op jit(solution)/shard_map/jit(cholesky)/cholesky | solution.py:44
  438.4 0.2 constant_dynamic-update-slice_fusion.1
  438.7 0.3 convolution_subtract_fusion
  438.9 11.9 %cholesky.111 = f32[128,128]{1,0:T(8,128)S(1)} custom-call(f32[128,128]{1,0:T(8,128)S(1)} %convolution_subtract_fusion), custom_call_target="Cholesky" | custom-call | tf_op jit(solution)/shard_map/jit(cholesky)/cholesky | solution.py:44
  450.9 0.6 compare_reduce_fusion
  452.9 9.8 %custom-call.15 = f32[1,128,128]{1,2,0:T(8,128)S(1)} custom-call(f32[1,128,128]{2,1,0:T(8,128)S(1)} %fusion.14), custom_call_target="InvertDiagBlocksLowerTriangular" | custom-call | tf_op jit(solution)/shard_map/triangular_solve | solution.py:46
  462.7 9.1 %fusion.17 = f32[128,16384]{1,0:T(8,128)} fusion(bf16[128,16384]{0,1:T(8,128)(2,1)} %bitcast.44, f32[1,128,128]{1,2,0:T(8,128)S(1)} %custom-call.15), kind=kOutput, calls=%fused_computation.25 | convolution fusion | flops 3221225472 | bytes 12648448 | tf_op jit(solution)/shard_map/triangular_solve | solution.py:46
  (40 shorter events, 1.4 us)
Async XLA Ops:
  7.2 28.5 %copy-start = (bf16[4,128,512]{2,1,0:T(8,128)(2,1)S(1)}, bf16[4,128,512]{2,1,0:T(8,128)(2,1)}, u32[]{:S(2)}) copy-start(bf16[4,128,512]{2,1,0:T(8,128)(2,1)} %param.11) | copy-start | bytes 1572868
  7.2 8.4 %copy-start.5 = (s32[32]{0:T(128)S(1)}, s32[32]{0:T(128)}, u32[]{:S(2)}) copy-start(s32[32]{0:T(128)} %param.8) | copy-start | bytes 388
  18.9 16.4 %copy-start.4 = (s32[32,4]{0,1:T(4,128)S(1)}, s32[32,4]{0,1:T(4,128)}, u32[]{:S(2)}) copy-start(s32[32,4]{0,1:T(4,128)} %param.9) | copy-start | bytes 1540
  18.9 16.6 %copy-start.3 = (s32[32,4]{0,1:T(4,128)S(1)}, s32[32,4]{0,1:T(4,128)}, u32[]{:S(2)}) copy-start(s32[32,4]{0,1:T(4,128)} %param.10) | copy-start | bytes 1540
  23.6 108.6 %all-to-all-start = ((bf16[256,64,128]{2,0,1:T(8,128)(2,1)}), bf16[256,64,128]{2,0,1:T(8,128)(2,1)}, u32[]{:S(2)}, u32[]{:S(2)}) async-start(bf16[256,64,128]{2,0,1:T(8,128)(2,1)} %multiply_bitcast_fusion), calls=%async_computation | async-start | bytes 8388608 | tf_op jit(solution)/shard_map/all_to_all | solution.py:36
  35.2 379.5 %all-reduce.3.cloned.1.call-start = ((), (), s32[]{:S(2)}) async-start(), calls=%async_computation.1 | async-start | bytes 524288 | tf_op jit(solution)/shard_map/psum | solution.py:42
  163.8 307.9 %copy-start.1 = (bf16[4,128,512]{2,1,0:T(8,128)(2,1)S(1)}, bf16[4,128,512]{2,1,0:T(8,128)(2,1)}, u32[]{:S(2)}) copy-start(bf16[4,128,512]{2,1,0:T(8,128)(2,1)} %param.11) | copy-start | bytes 1572868
  452.9 18.9 %copy-start.2 = (f32[256,256]{1,0:T(8,128)}, f32[256,256]{1,0:T(8,128)S(1)}, u32[]{:S(2)}) copy-start(f32[256,256]{1,0:T(8,128)S(1)} %select_select_fusion) | copy-start | bytes 786436
Sparse Core Ops, SparseCore 0:
  163.9 250.7 all-reduce.2
where the time goes:
time: 480 us; the launch traced here: 479 us
  waiting for transfers between devices  312 us (65%)
  local copies, waits for them, and re-layouts  56.6 us (12%)
  other arithmetic  50.8 us (11%)
  matrix products  32.2 us (7%)
  between operations  15.5 us (3%)
  starting transfers between devices  11.7 us (2%)
    psum x1, waiting for transfers between devices, body(): gram = lax.psum(gram, ('gx', 'gy'))  246 us
    all_to_all x1, waiting for transfers between devices, body(): lax.all_to_all(outgoing, 'gy', split_axis=1, concat_axis=1, tiled=True)  65.5 us
    another operation x6, other arithmetic, body(): factor = jnp.linalg.cholesky(covariance)  34.2 us
    gather x2, local copies, waits for them, and re-layouts, lift(): chosen = jnp.take(maps, levels, axis=0)  30.7 us
    dot_general x1, matrix products, lift(): jnp.einsum('sbnc,bncd->sbd', picked, chosen, preferred_element_type=jnp.f...  12.8 us
    all_to_all x1, starting transfers between devices, body(): lax.all_to_all(outgoing, 'gy', split_axis=1, concat_axis=1, tiled=True)  11.6 us
    dot_general x1, matrix products, body(): lax.dot_general(bricks, bricks, (((1,), (1,)), ((), ())), preferred_eleme...  9.83 us
    another operation x2, other arithmetic, body(): lax.linalg.triangular_solve(factor[:kept, :kept], bricks[:kept].astype(jn...  9.82 us
  transfers between devices with their start and end apart: 2, of which 2 were waited for; matrix products, arithmetic and copies ran while one was open for 8% of the time, Pallas kernels for 0%

commit v1 on v0

--- a/solution.py
+++ b/solution.py
@@ -2,6 +2,7 @@
 import jax.numpy as jnp
 from jax import lax
 from jax.sharding import PartitionSpec as P
+from jax.lax import all_gather
 
 RANK = 128
 BLK = 128
@@ -39,7 +40,8 @@
         bricks, bricks, (((1,), (1,)), ((), ())), preferred_element_type=jnp.float32
     )
     total_cells = lax.axis_size("gx") * lax.axis_size("gy") * bricks.shape[1]
-    gram = lax.psum(gram, ("gx", "gy"))
+    save_meshes = lambda base_x: jnp.sum(all_gather(base_x, ("gx", "gy")), axis=0)
+    gram = save_meshes(gram)
     covariance = gram / total_cells
     factor = jnp.linalg.cholesky(covariance)
     kept = RANK

time: 480 us -> 457 us (0.952)
  waiting for transfers between devices: 312 us -> 270 us
  other arithmetic: 50.8 us -> 70.8 us
    psum x1 -> x0, waiting for transfers between devices: 246 us -> none  [body(): gram = lax.psum(gram, ('gx', 'gy'))]
    all_gather x0 -> x1, waiting for transfers between devices: none -> 204 us  [body(): all_gather(base_x, ('gx', 'gy'))]
    reduce_sum x0 -> x1, other arithmetic: none -> 21.3 us  [body(): jnp.sum(all_gather(base_x, ('gx', 'gy')), axis=0)]
where the time goes in v1:
time: 457 us; the launch traced here: 455 us
  waiting for transfers between devices  270 us (59%)
  other arithmetic  70.8 us (15%)
  local copies, waits for them, and re-layouts  56.5 us (12%)
  matrix products  31.2 us (7%)
  between operations  15.5 us (3%)
  starting transfers between devices  11.7 us (3%)
    all_gather x1, waiting for transfers between devices, body(): all_gather(base_x, ('gx', 'gy'))  204 us
    all_to_all x1, waiting for transfers between devices, body(): lax.all_to_all(outgoing, 'gy', split_axis=1, concat_axis=1, tiled=True)  65.6 us
    another operation x6, other arithmetic, body(): factor = jnp.linalg.cholesky(covariance)  33.9 us
    gather x2, local copies, waits for them, and re-layouts, lift(): chosen = jnp.take(maps, levels, axis=0)  30.7 us
    reduce_sum x1, other arithmetic, body(): jnp.sum(all_gather(base_x, ('gx', 'gy')), axis=0)  21.3 us
    dot_general x1, matrix products, lift(): jnp.einsum('sbnc,bncd->sbd', picked, chosen, preferred_element_type=jnp.f...  12.8 us
    all_to_all x1, starting transfers between devices, body(): lax.all_to_all(outgoing, 'gy', split_axis=1, concat_axis=1, tiled=True)  11.6 us
    another operation x2, other arithmetic, body(): lax.linalg.triangular_solve(factor[:kept, :kept], bricks[:kept].astype(jn...  10 us
  transfers between devices with their start and end apart: 2, of which 2 were waited for; matrix products, arithmetic and copies ran while one was open for 8% of the time, Pallas kernels for 0%

profile of v1, /device:TPU:2, one launch (start us, length us, event | category | flops | bytes accessed | tf_op | source)
XLA Modules:
  0.0 455.2 jit_solution(18167191509244958377)
XLA Ops:
  7.2 0.8 copy.45
  8.2 0.7 fusion.20
  9.1 4.1 copy.46
  13.2 3.2 copy.48
  16.4 3.1 gather_fusion.1
  19.5 4.7 %multiply_bitcast_fusion = bf16[256,64,128]{2,0,1:T(8,128)(2,1)} fusion(bf16[64,256,128]{2,1,0:T(8,128)(2,1)} %gather_fusion.1, pred[64]{0:T(512)(128)(4,1)S(1)} %compare_and_fusion, bf16[64]{0:T(256)(128)(2,1)S(1)} %reshape.98), kind=kLoop, calls=%fused_computation.12 | loop fusion | flops 4194304 | bytes 8388800 | tf_op jit(solution)/shard_map/mul | solution.py:36
  24.2 11.6 %all-to-all-start = ((bf16[256,64,128]{2,0,1:T(8,128)(2,1)}), bf16[256,64,128]{2,0,1:T(8,128)(2,1)}, u32[]{:S(2)}, u32[]{:S(2)}) async-start(bf16[256,64,128]{2,0,1:T(8,128)(2,1)} %multiply_bitcast_fusion), calls=%async_computation | async-start | bytes 8388608 | tf_op jit(solution)/shard_map/all_to_all | solution.py:37
  36.6 8.1 %gather_fusion = bf16[128,128,512]{2,1,0:T(8,128)(2,1)} fusion(bf16[4,128,512]{2,1,0:T(8,128)(2,1)S(1)} %copy-done, s32[1024]{0:T(1024)S(1)} %pad_clamp_fusion.2), kind=kCustom, calls=%fused_computation | custom fusion | bytes 33554944 | tf_op jit(solution)/shard_map/jit(_take)/gather | solution.py:19
  44.7 22.5 %copy.43 = bf16[32,4,128,512]{2,3,1,0:T(8,128)(2,1)} copy(bf16[32,4,128,512]{3,2,1,0:T(8,128)(2,1)} %bitcast.44) | data formatting | bytes 33554432 | tf_op jit(solution)/shard_map/jit(_take)/gather | solution.py:19
  67.2 65.6 %all-to-all-done = bf16[256,64,128]{2,0,1:T(8,128)(2,1)} async-done(((bf16[256,64,128]{2,0,1:T(8,128)(2,1)}), bf16[256,64,128]{2,0,1:T(8,128)(2,1)}, u32[]{:S(2)}, u32[]{:S(2)}) %all-to-all-start) | async-done | bytes 4194336 | tf_op jit(solution)/shard_map/all_to_all | solution.py:37
  132.8 8.9 %gather_fusion.2 = bf16[128,256,128]{2,1,0:T(8,128)(2,1)} fusion(bf16[256,64,128]{2,0,1:T(8,128)(2,1)} %all-to-all-done, s32[1024]{0:T(1024)S(1)} %pad_clamp_fusion), kind=kCustom, calls=%fused_computation.2 | custom fusion | bytes 16777728 | tf_op jit(solution)/shard_map/jit(_take)/gather | solution.py:18
  141.8 12.8 %fusion.3 = bf16[256,32,512]{0,2,1:T(8,128)(2,1)} fusion(bf16[32,4,256,128]{3,2,1,0:T(8,128)(2,1)} %bitcast.46, pred[32,4]{1,0:T(8,128)(4,1)S(1)} %copy.44, bf16[32,4,128,512]{2,3,1,0:T(8,128)(2,1)} %copy.43, pred[32,4]{1,0:T(8,128)(4,1)S(1)} %copy.41), kind=kOutput, calls=%fused_computation.7 | convolution fusion | flops 4311744512 | bytes 33554688 | tf_op jit(solution)/shard_map/sbnc,bncd->sbd/dot_general | solution.py:20
  154.6 8.8 %convolution_bitcast_fusion = f32[256,256]{1,0:T(8,128)} fusion(bf16[256,32,512]{0,2,1:T(8,128)(2,1)} %fusion.3), kind=kOutput, calls=%fused_computation.14 | convolution fusion | flops 2147483648 | bytes 8650752 | tf_op jit(solution)/shard_map/dot_general | solution.py:39
  163.4 4.6 %triangular_solve.20 = bf16[128,32,512]{0,2,1:T(8,128)(2,1)} slice(bf16[256,32,512]{0,2,1:T(8,128)(2,1)} %fusion.3), slice={[0:128], [0:32], [0:512]} | slice | bytes 8388608 | tf_op jit(solution)/shard_map/triangular_solve | solution.py:48
  168.0 203.9 %all-gather.3.cloned.1.call-done = f32[65536,256]{1,0:T(8,128)} async-done(((f32[256,256]{1,0:T(8,128)}), f32[65536,256]{1,0:T(8,128)}) %all-gather.3.cloned.1.call-update) | async-done | bytes 67108880 | tf_op jit(solution)/shard_map/all_gather | solution.py:43
  372.0 21.3 %reduce_sum.11 = f32[256,256]{1,0:T(8,128)S(1)} reduce(f32[256,256,256]{2,1,0:T(8,128)} %bitcast.10, f32[]{:T(128)} %constant.117.clone.1), dimensions={0}, to_apply=%region_0.1 | reduce | flops 16711680 | bytes 67371008 | tf_op jit(solution)/shard_map/reduce_sum | solution.py:43
  393.4 11.7 %cholesky.53 = f32[128,128]{1,0:T(8,128)S(1)} custom-call(f32[128,128]{1,0:T(8,128)S(1)} %cholesky.124), custom_call_target="Cholesky" | custom-call | tf_op jit(solution)/shard_map/jit(cholesky)/cholesky | solution.py:46
  405.2 9.8 %custom-call.14 = f32[1,128,128]{1,2,0:T(8,128)S(1)} custom-call(f32[1,128,128]{2,1,0:T(8,128)S(1)} %get-tuple-element.5), custom_call_target="InvertDiagBlocksLowerTriangular" | custom-call | tf_op jit(solution)/shard_map/jit(cholesky)/cholesky | solution.py:46
  415.0 0.2 constant_dynamic-update-slice_fusion.1
  415.2 0.3 convolution_subtract_fusion
  415.5 11.7 %cholesky.111 = f32[128,128]{1,0:T(8,128)S(1)} custom-call(f32[128,128]{1,0:T(8,128)S(1)} %convolution_subtract_fusion), custom_call_target="Cholesky" | custom-call | tf_op jit(solution)/shard_map/jit(cholesky)/cholesky | solution.py:46
  427.2 0.6 compare_reduce_fusion
  429.3 10.0 %custom-call.15 = f32[1,128,128]{1,2,0:T(8,128)S(1)} custom-call(f32[1,128,128]{2,1,0:T(8,128)S(1)} %fusion.14), custom_call_target="InvertDiagBlocksLowerTriangular" | custom-call | tf_op jit(solution)/shard_map/triangular_solve | solution.py:48
  439.3 9.1 %fusion.17 = f32[128,16384]{1,0:T(8,128)} fusion(bf16[128,16384]{0,1:T(8,128)(2,1)} %bitcast.45, f32[1,128,128]{1,2,0:T(8,128)S(1)} %custom-call.15), kind=kOutput, calls=%fused_computation.24 | convolution fusion | flops 3221225472 | bytes 12648448 | tf_op jit(solution)/shard_map/triangular_solve | solution.py:48
  (38 shorter events, 1.4 us)
Async XLA Ops:
  7.2 29.4 %copy-start = (bf16[4,128,512]{2,1,0:T(8,128)(2,1)S(1)}, bf16[4,128,512]{2,1,0:T(8,128)(2,1)}, u32[]{:S(2)}) copy-start(bf16[4,128,512]{2,1,0:T(8,128)(2,1)} %param.11) | copy-start | bytes 1572868
  19.5 16.4 %copy-start.3 = (s32[32,4]{0,1:T(4,128)S(1)}, s32[32,4]{0,1:T(4,128)}, u32[]{:S(2)}) copy-start(s32[32,4]{0,1:T(4,128)} %param.10) | copy-start | bytes 1540
  19.5 16.5 %copy-start.4 = (s32[32,4]{0,1:T(4,128)S(1)}, s32[32,4]{0,1:T(4,128)}, u32[]{:S(2)}) copy-start(s32[32,4]{0,1:T(4,128)} %param.9) | copy-start | bytes 1540
  24.2 108.6 %all-to-all-start = ((bf16[256,64,128]{2,0,1:T(8,128)(2,1)}), bf16[256,64,128]{2,0,1:T(8,128)(2,1)}, u32[]{:S(2)}, u32[]{:S(2)}) async-start(bf16[256,64,128]{2,0,1:T(8,128)(2,1)} %multiply_bitcast_fusion), calls=%async_computation | async-start | bytes 8388608 | tf_op jit(solution)/shard_map/all_to_all | solution.py:37
  35.8 336.1 %all-gather.3.cloned.1.call-start = ((), (), s32[]{:S(2)}) async-start(), calls=%async_computation.1 | async-start | bytes 67371008 | tf_op jit(solution)/shard_map/all_gather | solution.py:43
  372.0 76.4 %copy-start.1 = (bf16[4,128,512]{2,1,0:T(8,128)(2,1)S(1)}, bf16[4,128,512]{2,1,0:T(8,128)(2,1)}, u32[]{:S(2)}) copy-start(bf16[4,128,512]{2,1,0:T(8,128)(2,1)} %param.11) | copy-start | bytes 1572868
  429.2 19.1 %copy-start.2 = (f32[256,256]{1,0:T(8,128)}, f32[256,256]{1,0:T(8,128)S(1)}, u32[]{:S(2)}) copy-start(f32[256,256]{1,0:T(8,128)S(1)} %select_select_fusion) | copy-start | bytes 786436
Sparse Core Ops, SparseCore 0:
  163.6 208.3 all-gather.2
